TPU v7x, 32 devices: a whole 2x2x4 slice. The times are simulated.
32 devices in a mesh: dp: 4 (over y, core), freq: 8 (over z, x).
Axes of the slice: x: 2, y: 2, z: 4, core: 2. Of those that a mesh axis runs over, the one named last changes fastest.
Arguments:
- grad_parts: float32 [4, 27, 4, 65536], P('dp', None, None, 'freq'), may hold values from -12 to 12
- kernel: float32 [27, 262144], P(None, ('dp', 'freq')), may hold values from -4 to 4
Outputs:
- clipped: float32 [27, 262144], P(None, ('dp', 'freq'))
All inputs are finite; a program needn't handle non-finite values.
Results may differ from a plain program's by a relative error of at most 0.0005.
The roundings to bfloat16 on the way count: a program that leaves them out, or rounds other values in their place, can miss the bound.
Values may be sent and summed in bfloat16 or wider, within the bound.
No kernel may reach another device: no remote copies, remote signals or barrier semaphores. Data moves between devices by JAX's collectives and lax.ppermute only.
A program may use at most 64 MiB of HBM per device.

v0:
```python
import math
import jax
import jax.numpy as jnp
from jax import lax
from jax.sharding import PartitionSpec as P

C = 512
TAPS = 27
GT = 8
GH = 32
GW = 32
KD = 2
CLIP = 0.25
HIGH = lax.Precision.HIGHEST


def tap_phases(freq_ids, stride):
    flat_index = freq_ids * stride
    freq_time = flat_index // (GH * GW)
    freq_row = flat_index // GW % GH
    freq_col = flat_index % GW
    taps = jnp.arange(TAPS, dtype=jnp.int32)
    off_time = taps // 9 - 1
    off_row = taps // 3 % 3 - 1
    off_col = taps % 3 - 1
    period = GT * GH * GW
    turns = (
        freq_time[:, None] * off_time[None, :] * (GH * GW)
        + freq_row[:, None] * off_row[None, :] * (GT * GW)
        + freq_col[:, None] * off_col[None, :] * (GT * GH)
    ) % period
    angle = turns.astype(jnp.float32) * (2.0 * math.pi / period)
    return (jnp.cos(angle), jnp.sin(angle))


def clip_factor(local_square):
    summed = lax.psum(local_square, ("dp", "freq"))
    return jnp.minimum(1.0, CLIP * math.sqrt(TAPS * C * C) / jnp.sqrt(summed + 1e-06))


def spectrum(field, cosine, sine_rows):
    real_spec = jnp.dot(cosine, field, precision=HIGH)
    imag_spec = -jnp.dot(sine_rows, field, precision=HIGH)
    return jnp.stack([real_spec, imag_spec], axis=1)


def taps_back(polar_part, cosine, sine_rows):
    values = polar_part.astype(jnp.float32)
    summed = jnp.dot(cosine.T, values[:, 0], precision=HIGH)
    return summed - jnp.dot(sine_rows.T, values[:, 1], precision=HIGH)


def polar_step(spectra):
    width = spectra.shape[-1]
    mean_square = jnp.mean(jnp.square(spectra.astype(jnp.float32)), axis=(1, 2, 3), keepdims=True)
    spread = math.sqrt(8.0 * width)
    scaled = (
        spectra.astype(jnp.float32) * (0.75 / (spread * jnp.sqrt(mean_square + 1e-06)))
    ).astype(jnp.bfloat16)
    real_part = scaled[:, 0]
    imag_part = scaled[:, 1]
    stacked = jnp.concatenate([real_part, imag_part], axis=1)
    turned = jnp.concatenate([imag_part, -real_part], axis=1)
    gram = jnp.einsum(
        "nri,nrj->nij",
        stacked,
        jnp.concatenate([stacked, turned], axis=2),
        preferred_element_type=jnp.float32,
    ).astype(jnp.bfloat16)
    gram_real = gram[:, :, :width]
    gram_imag = gram[:, :, width:]
    blocked = jnp.concatenate([gram, jnp.concatenate([-gram_imag, gram_real], axis=2)], axis=1)
    side = jnp.concatenate([real_part, imag_part], axis=2)
    product = jnp.einsum("nij,njk->nik", side, blocked, preferred_element_type=jnp.float32)
    result = (1.5 * side.astype(jnp.float32) - 0.5 * product).astype(jnp.bfloat16)
    return jnp.stack([result[:, :, :width], result[:, :, width:]], axis=1)


def on_device(grad_parts, kernel):
    devices_dp = lax.axis_size("dp")
    devices_freq = lax.axis_size("freq")
    total_freq = KD * devices_dp * devices_freq
    stride = GT * GH * GW // total_freq
    scale_out = math.sqrt(C / total_freq)
    own_width = kernel.shape[1]
    gradient = lax.psum_scatter(grad_parts[0], "dp", scatter_dimension=1, tiled=True).reshape(
        TAPS, own_width
    )
    local_square = jnp.sum(gradient * gradient)
    kernel_all, gradient_all = (kernel, gradient)
    freq_ids = jnp.arange(total_freq, dtype=jnp.int32)
    cosine, sine_rows = tap_phases(freq_ids, stride)
    factor = clip_factor(local_square)
    spectra = spectrum(kernel_all - factor * gradient_all, cosine, sine_rows)
    spectra = spectra.astype(jnp.bfloat16)
    count, row_width = (spectra.shape[0], spectra.shape[2])
    whole = lax.all_to_all(
        lax.all_to_all(
            spectra.reshape(count, 2, 1, 1, row_width),
            "dp",
            split_axis=0,
            concat_axis=2,
            tiled=True,
        ),
        "freq",
        split_axis=0,
        concat_axis=3,
        tiled=True,
    )
    polar_part = polar_step(whole.reshape(KD, 2, C, C))
    returned = lax.all_to_all(
        lax.all_to_all(
            polar_part.reshape(KD, 2, devices_dp, devices_freq, row_width),
            "dp",
            split_axis=2,
            concat_axis=0,
            tiled=True,
        ),
        "freq",
        split_axis=3,
        concat_axis=0,
        tiled=True,
    )
    position = jnp.arange(total_freq, dtype=jnp.int32)
    source_freq = position // (devices_dp * KD)
    source_dp = position // KD % devices_dp
    member = position % KD
    back_ids = source_dp * (devices_freq * KD) + source_freq * KD + member
    back_cos, back_sin = tap_phases(back_ids, stride)
    return taps_back(returned.reshape(count, 2, row_width), back_cos, back_sin) * scale_out


def solution(mesh):
    return jax.shard_map(
        on_device,
        mesh=mesh,
        in_specs=(P("dp", None, None, "freq"), P(None, ("dp", "freq"))),
        out_specs=P(None, ("dp", "freq")),
        check_vma=False,
    )
```

profile of v0, /device:TPU:0, one launch (start us, length us, event | category | flops | bytes accessed | tf_op | source)
XLA Modules:
  0.0 307.9 jit_solution(1594015570563499403)
XLA Ops:
  6.5 0.0 reduce-scatter.2.cloned.1.call-start
  6.5 6.0 %copy.47 = f32[1,27,4,8192]{3,1,2,0:T(8,128)} copy(f32[1,27,4,8192]{3,2,1,0:T(4,128)} %param.2) | data formatting | bytes 7077888 | tf_op args[0]
  12.5 0.0 copy-start.1
  12.5 0.0 reduce-scatter.2.cloned.1.call-update
  12.6 47.3 %reduce-scatter.2.cloned.1.call-done = f32[27,1,8192]{2,0,1:T(8,128)} async-done(((f32[27,4,8192]{2,0,1:T(8,128)}), f32[27,1,8192]{2,0,1:T(8,128)}) %reduce-scatter.2.cloned.1.call-update) | async-done | bytes 884752 | tf_op jit(solution)/shard_map/reduce_scatter | solution.py:86
  59.9 0.0 copy-start
  59.9 2.2 multiply_reduce_fusion.1
  62.1 39.5 %psum.7 = f32[]{:T(128)} all-reduce(f32[]{:T(128)} %multiply_reduce_fusion.1), channel_id=1, replica_groups=mesh['dp'=4,'freq'=8] {'dp','freq'}, use_global_device_ids=true, to_apply=%region_2.3 | all-reduce | flops 1 | bytes 8 | tf_op jit(solution)/shard_map/psum | solution.py:37
  102.3 0.0 copy-done.1
  102.3 3.2 %fusion.2 = bf16[64,1,1,1,8192]{4,0,3,2,1:T(8,128)(2,1)S(1)} fusion(f32[27,8192]{1,0:T(8,128)S(1)} %copy-done.1, f32[27,1,8192]{2,0,1:T(8,128)} %reduce-scatter.2.cloned.1.call-done, f32[]{:T(128)S(6)} %min_shard_map.3, s32[64]{0:T(128)S(1)} %get-tuple-element.11, s32[64]{0:T(128)S(1)} %get-tuple-element.12, s32[64]{0:T(128)S(1)} %and_select_fusion.3, ...), kind=kOutput, calls=%fused_computation.4 | convolution fusion | flops 171396544 | bytes 2819144 | tf_op jit(solution)/shard_map/dot_general | solution.py:43
  105.6 0.0 copy-done
  105.6 2.0 fusion.1
  107.6 0.2 pad_maximum_fusion
  107.8 2.2 copy.32
  110.0 29.2 %all_to_all.60 = bf16[64,2,1,1,8192]{4,1,3,2,0:T(2,128)(2,1)S(1)} all-to-all(bf16[64,2,1,1,8192]{4,1,3,2,0:T(2,128)(2,1)S(1)} %copy.32), channel_id=1, replica_groups=mesh['dp'=4,'freq'=8] {'dp'}, dimensions={0} | all-to-all | bytes 4194304 | tf_op jit(solution)/shard_map/all_to_all | solution.py:98
  139.2 1.2 copy.33
  140.4 1.6 copy.34
  142.0 52.3 %all_to_all.61 = bf16[16,2,4,1,8192]{4,2,1,3,0:T(4,128)(2,1)S(1)} all-to-all(bf16[16,2,4,1,8192]{4,2,1,3,0:T(4,128)(2,1)S(1)} %copy.34), channel_id=1, replica_groups=mesh['dp'=4,'freq'=8] {'freq'}, dimensions={0} | all-to-all | bytes 4194304 | tf_op jit(solution)/shard_map/all_to_all | solution.py:97
  194.3 1.2 multiply_reduce_fusion
  195.6 0.1 reduce_sum.27
  195.7 3.2 %copy.46 = f32[8,2,2,4,1,8192]{5,0,3,1,2,4:T(8,128)} copy(bf16[8,2,2,4,1,8192]{5,3,2,1,0,4:T(4,128)(2,1)S(1)} %bitcast.49) | data formatting | bytes 6291456 | tf_op jit(solution)/shard_map/convert_element_type | solution.py:58
  198.8 5.0 %reshape.259 = f32[2,2,512,512]{3,2,0,1:T(8,128)} reshape(f32[2,2,4,8,1,8192]{5,3,2,0,1,4:T(8,128)} %bitcast.50) | data formatting | bytes 8388608 | tf_op jit(solution)/shard_map/convert_element_type | solution.py:58
  203.8 2.8 multiply_convert_fusion
  206.6 0.1 fusion.83
  206.7 0.1 slice_bitcast_fusion.5
  206.9 2.6 fusion.23
  209.5 0.1 slice_negate_fusion
  209.6 2.6 subtract_convert_fusion
  212.2 0.2 fusion.84
  212.4 0.5 stack.21
  212.9 0.5 stack.22
  213.5 0.2 pad_maximum_fusion.2
  213.7 0.2 copy.42
  213.9 28.2 %all_to_all.62 = bf16[2,2,4,8,8192]{4,3,1,0,2:T(8,128)(2,1)S(1)} all-to-all(bf16[2,2,4,8,8192]{4,3,1,0,2:T(8,128)(2,1)S(1)} %copy.42), channel_id=1, replica_groups=mesh['dp'=4,'freq'=8] {'dp'}, dimensions={2} | all-to-all | bytes 4194304 | tf_op jit(solution)/shard_map/all_to_all | solution.py:112
  242.0 3.5 %copy.39 = bf16[8,2,1,8,8192]{4,1,0,2,3:T(2,128)(2,1)} copy(bf16[8,2,1,8,8192]{4,3,1,0,2:T(8,128)(2,1)S(1)} %bitcast.55) | data formatting | bytes 4194304 | tf_op jit(solution)/shard_map/all_to_all | solution.py:112
  245.6 3.6 %all-to-all-start.3 = ((bf16[8,2,1,8,8192]{4,1,0,2,3:T(2,128)(2,1)}), bf16[8,2,1,8,8192]{4,1,0,2,3:T(2,128)(2,1)S(1)}, u32[]{:S(2)}, u32[]{:S(2)}) async-start(bf16[8,2,1,8,8192]{4,1,0,2,3:T(2,128)(2,1)} %copy.39), calls=%async_computation.4 | async-start | bytes 4194304 | tf_op jit(solution)/shard_map/all_to_all | solution.py:111
  249.2 48.0 %all-to-all-done.3 = bf16[8,2,1,8,8192]{4,1,0,2,3:T(2,128)(2,1)S(1)} async-done(((bf16[8,2,1,8,8192]{4,1,0,2,3:T(2,128)(2,1)}), bf16[8,2,1,8,8192]{4,1,0,2,3:T(2,128)(2,1)S(1)}, u32[]{:S(2)}, u32[]{:S(2)}) %all-to-all-start.3) | async-done | bytes 2097184 | tf_op jit(solution)/shard_map/all_to_all | solution.py:111
  297.2 1.2 copy.48
  298.4 0.8 fusion.28
  299.2 1.8 fusion.3
  (8 shorter events, 0.1 us)
Async XLA Ops:
  6.5 53.4 %reduce-scatter.2.cloned.1.call-start = ((), (), s32[]{:S(2)}) async-start(), calls=%async_computation.5 | async-start | bytes 5242880 | tf_op jit(solution)/shard_map/reduce_scatter | solution.py:86
  12.5 89.8 %copy-start.1 = (f32[27,8192]{1,0:T(8,128)S(1)}, f32[27,8192]{1,0:T(8,128)}, u32[]{:S(2)}) copy-start(f32[27,8192]{1,0:T(8,128)} %param.3) | copy-start | bytes 2654212
  59.9 45.7 %copy-start = (f32[27,1,8192]{2,0,1:T(8,128)S(1)}, f32[27,1,8192]{2,0,1:T(8,128)}, u32[]{:S(2)}) copy-start(f32[27,1,8192]{2,0,1:T(8,128)} %reduce-scatter.2.cloned.1.call-done) | copy-start | bytes 2654212
  245.6 51.7 %all-to-all-start.3 = ((bf16[8,2,1,8,8192]{4,1,0,2,3:T(2,128)(2,1)}), bf16[8,2,1,8,8192]{4,1,0,2,3:T(2,128)(2,1)S(1)}, u32[]{:S(2)}, u32[]{:S(2)}) async-start(bf16[8,2,1,8,8192]{4,1,0,2,3:T(2,128)(2,1)} %copy.39), calls=%async_computation.4 | async-start | bytes 4194304 | tf_op jit(solution)/shard_map/all_to_all | solution.py:111
Sparse Core Ops, SparseCore 0:
  12.7 47.2 reduce-scatter.1
where the time goes:
time: 308 us
  blocking collectives  149 us (48%)
  waiting for transfers between devices  95.4 us (31%)
  local copies, waits for them, and re-layouts  25.4 us (8%)
  between operations  14.3 us (5%)
  matrix products  13 us (4%)
  other arithmetic  6.98 us (2%)
  starting transfers between devices  3.6 us (1%)
    all_to_all x1, blocking collectives, on_device(): lax.all_to_all(lax.all_to_all(spectra.reshape(count, 2, 1, 1, row_width),...  52.3 us
    all_to_all x1, waiting for transfers between devices, on_device(): lax.all_to_all(lax.all_to_all(polar_part.reshape(KD, 2, devices_dp, devic...  48 us
    reduce_scatter x1, waiting for transfers between devices, on_device(): lax.psum_scatter(grad_parts[0], 'dp', scatter_dimension=1, tiled=True)  47.3 us
    psum x1, blocking collectives, clip_factor(): summed = lax.psum(local_square, ('dp', 'freq'))  39.5 us
    all_to_all x1, blocking collectives, on_device(): lax.all_to_all(spectra.reshape(count, 2, 1, 1, row_width), 'dp', split_ax...  29.2 us
    all_to_all x1, blocking collectives, on_device(): lax.all_to_all(polar_part.reshape(KD, 2, devices_dp, devices_freq, row_wi...  28.2 us
    convert_element_type x2, local copies, waits for them, and re-layouts, polar_step(): spectra.astype(jnp.float32)  8.14 us
  transfers between devices with their start and end apart: 2, of which 2 were waited for; matrix products, arithmetic and copies ran while one was open for 0% of the time, Pallas kernels for 0%

commit v1 on v0

--- a/solution.py
+++ b/solution.py
@@ -34,7 +34,7 @@
 
 
 def clip_factor(local_square):
-    summed = lax.psum(local_square, ("dp", "freq"))
+    summed = lax.psum(lax.psum(local_square, "freq"), "dp")
     return jnp.minimum(1.0, CLIP * math.sqrt(TAPS * C * C) / jnp.sqrt(summed + 1e-06))
 
 

time: 308 us -> 295 us (0.958)
  blocking collectives: 149 us -> 135 us
    psum x1 -> x2, blocking collectives: 39.5 us -> 28.5 us  [clip_factor(): summed = lax.psum(lax.psum(local_square, 'freq'), 'dp')]
where the time goes in v1:
time: 295 us; the launch traced here: 294 us
  blocking collectives  135 us (46%)
  waiting for transfers between devices  95.4 us (32%)
  local copies, waits for them, and re-layouts  25.4 us (9%)
  between operations  14.3 us (5%)
  matrix products  13 us (4%)
  other arithmetic  6.98 us (2%)
  starting transfers between devices  3.6 us (1%)
    all_to_all x1, blocking collectives, on_device(): lax.all_to_all(lax.all_to_all(spectra.reshape(count, 2, 1, 1, row_width),...  50.6 us
    all_to_all x1, waiting for transfers between devices, on_device(): lax.all_to_all(lax.all_to_all(polar_part.reshape(KD, 2, devices_dp, devic...  48 us
    reduce_scatter x1, waiting for transfers between devices, on_device(): lax.psum_scatter(grad_parts[0], 'dp', scatter_dimension=1, tiled=True)  47.3 us
    psum x2, blocking collectives, clip_factor(): summed = lax.psum(lax.psum(local_square, 'freq'), 'dp')  28.5 us
    all_to_all x1, blocking collectives, on_device(): lax.all_to_all(spectra.reshape(count, 2, 1, 1, row_width), 'dp', split_ax...  28.2 us
    all_to_all x1, blocking collectives, on_device(): lax.all_to_all(polar_part.reshape(KD, 2, devices_dp, devices_freq, row_wi...  28.2 us
    convert_element_type x2, local copies, waits for them, and re-layouts, polar_step(): spectra.astype(jnp.float32)  8.14 us
    unnamed x5, local copies, waits for them, and re-layouts  5.99 us
  transfers between devices with their start and end apart: 2, of which 2 were waited for; matrix products, arithmetic and copies ran while one was open for 0% of the time, Pallas kernels for 0%

profile of v1, /device:TPU:0, one launch (start us, length us, event | category | flops | bytes accessed | tf_op | source)
XLA Modules:
  0.0 294.2 jit_solution(4403301753157289322)
XLA Ops:
  6.5 0.0 reduce-scatter.2.cloned.1.call-start
  6.5 6.0 %copy.47 = f32[1,27,4,8192]{3,1,2,0:T(8,128)} copy(f32[1,27,4,8192]{3,2,1,0:T(4,128)} %param.2) | data formatting | bytes 7077888 | tf_op args[0]
  12.5 0.0 copy-start.1
  12.5 0.0 reduce-scatter.2.cloned.1.call-update
  12.6 47.3 %reduce-scatter.2.cloned.1.call-done = f32[27,1,8192]{2,0,1:T(8,128)} async-done(((f32[27,4,8192]{2,0,1:T(8,128)}), f32[27,1,8192]{2,0,1:T(8,128)}) %reduce-scatter.2.cloned.1.call-update) | async-done | bytes 884752 | tf_op jit(solution)/shard_map/reduce_scatter | solution.py:86
  59.9 0.0 copy-start
  59.9 2.2 multiply_reduce_fusion.1
  62.1 22.0 %psum.14 = f32[]{:T(128)} all-reduce(f32[]{:T(128)} %multiply_reduce_fusion.1), channel_id=1, replica_groups=mesh['dp'=4,'freq'=8] {'freq'}, use_global_device_ids=true, to_apply=%region_2.3 | all-reduce | flops 1 | bytes 8 | tf_op jit(solution)/shard_map/psum | solution.py:37
  84.1 6.6 %psum.15 = f32[]{:T(128)} all-reduce(f32[]{:T(128)} %psum.14), channel_id=1, replica_groups=mesh['dp'=4,'freq'=8] {'dp'}, use_global_device_ids=true, to_apply=%region_3.4 | all-reduce | flops 1 | bytes 8 | tf_op jit(solution)/shard_map/psum | solution.py:37
  91.4 0.0 copy-done.1
  91.4 3.2 %fusion.2 = bf16[64,1,1,1,8192]{4,0,3,2,1:T(8,128)(2,1)S(1)} fusion(f32[27,8192]{1,0:T(8,128)S(1)} %copy-done.1, f32[27,1,8192]{2,0,1:T(8,128)} %reduce-scatter.2.cloned.1.call-done, f32[]{:T(128)S(6)} %min_shard_map.3, s32[64]{0:T(128)S(1)} %get-tuple-element.11, s32[64]{0:T(128)S(1)} %get-tuple-element.12, s32[64]{0:T(128)S(1)} %and_select_fusion.3, ...), kind=kOutput, calls=%fused_computation.4 | convolution fusion | flops 171396544 | bytes 2819144 | tf_op jit(solution)/shard_map/dot_general | solution.py:43
  94.6 0.0 copy-done
  94.6 2.0 fusion.1
  96.6 0.2 pad_maximum_fusion
  96.8 2.2 copy.32
  99.0 28.2 %all_to_all.60 = bf16[64,2,1,1,8192]{4,1,3,2,0:T(2,128)(2,1)S(1)} all-to-all(bf16[64,2,1,1,8192]{4,1,3,2,0:T(2,128)(2,1)S(1)} %copy.32), channel_id=1, replica_groups=mesh['dp'=4,'freq'=8] {'dp'}, dimensions={0} | all-to-all | bytes 4194304 | tf_op jit(solution)/shard_map/all_to_all | solution.py:98
  127.2 1.2 copy.33
  128.3 1.6 copy.34
  130.0 50.6 %all_to_all.61 = bf16[16,2,4,1,8192]{4,2,1,3,0:T(4,128)(2,1)S(1)} all-to-all(bf16[16,2,4,1,8192]{4,2,1,3,0:T(4,128)(2,1)S(1)} %copy.34), channel_id=1, replica_groups=mesh['dp'=4,'freq'=8] {'freq'}, dimensions={0} | all-to-all | bytes 4194304 | tf_op jit(solution)/shard_map/all_to_all | solution.py:97
  180.6 1.2 multiply_reduce_fusion
  181.8 0.1 reduce_sum.27
  181.9 3.2 %copy.46 = f32[8,2,2,4,1,8192]{5,0,3,1,2,4:T(8,128)} copy(bf16[8,2,2,4,1,8192]{5,3,2,1,0,4:T(4,128)(2,1)S(1)} %bitcast.49) | data formatting | bytes 6291456 | tf_op jit(solution)/shard_map/convert_element_type | solution.py:58
  185.1 5.0 %reshape.259 = f32[2,2,512,512]{3,2,0,1:T(8,128)} reshape(f32[2,2,4,8,1,8192]{5,3,2,0,1,4:T(8,128)} %bitcast.50) | data formatting | bytes 8388608 | tf_op jit(solution)/shard_map/convert_element_type | solution.py:58
  190.1 2.8 multiply_convert_fusion
  192.9 0.1 fusion.83
  193.0 0.1 slice_bitcast_fusion.5
  193.1 2.6 fusion.23
  195.7 0.1 slice_negate_fusion
  195.9 2.6 subtract_convert_fusion
  198.4 0.2 fusion.84
  198.6 0.5 stack.21
  199.2 0.5 stack.22
  199.7 0.2 pad_maximum_fusion.2
  199.9 0.2 copy.42
  200.1 28.2 %all_to_all.62 = bf16[2,2,4,8,8192]{4,3,1,0,2:T(8,128)(2,1)S(1)} all-to-all(bf16[2,2,4,8,8192]{4,3,1,0,2:T(8,128)(2,1)S(1)} %copy.42), channel_id=1, replica_groups=mesh['dp'=4,'freq'=8] {'dp'}, dimensions={2} | all-to-all | bytes 4194304 | tf_op jit(solution)/shard_map/all_to_all | solution.py:112
  228.3 3.5 %copy.39 = bf16[8,2,1,8,8192]{4,1,0,2,3:T(2,128)(2,1)} copy(bf16[8,2,1,8,8192]{4,3,1,0,2:T(8,128)(2,1)S(1)} %bitcast.55) | data formatting | bytes 4194304 | tf_op jit(solution)/shard_map/all_to_all | solution.py:112
  231.8 3.6 %all-to-all-start.3 = ((bf16[8,2,1,8,8192]{4,1,0,2,3:T(2,128)(2,1)}), bf16[8,2,1,8,8192]{4,1,0,2,3:T(2,128)(2,1)S(1)}, u32[]{:S(2)}, u32[]{:S(2)}) async-start(bf16[8,2,1,8,8192]{4,1,0,2,3:T(2,128)(2,1)} %copy.39), calls=%async_computation.4 | async-start | bytes 4194304 | tf_op jit(solution)/shard_map/all_to_all | solution.py:111
  235.5 48.0 %all-to-all-done.3 = bf16[8,2,1,8,8192]{4,1,0,2,3:T(2,128)(2,1)S(1)} async-done(((bf16[8,2,1,8,8192]{4,1,0,2,3:T(2,128)(2,1)}), bf16[8,2,1,8,8192]{4,1,0,2,3:T(2,128)(2,1)S(1)}, u32[]{:S(2)}, u32[]{:S(2)}) %all-to-all-start.3) | async-done | bytes 2097184 | tf_op jit(solution)/shard_map/all_to_all | solution.py:111
  283.5 1.2 copy.48
  284.7 0.8 fusion.28
  285.5 1.8 fusion.3
  (8 shorter events, 0.1 us)
Async XLA Ops:
  6.5 53.4 %reduce-scatter.2.cloned.1.call-start = ((), (), s32[]{:S(2)}) async-start(), calls=%async_computation.5 | async-start | bytes 5242880 | tf_op jit(solution)/shard_map/reduce_scatter | solution.py:86
  12.5 78.9 %copy-start.1 = (f32[27,8192]{1,0:T(8,128)S(1)}, f32[27,8192]{1,0:T(8,128)}, u32[]{:S(2)}) copy-start(f32[27,8192]{1,0:T(8,128)} %param.3) | copy-start | bytes 2654212
  59.9 34.7 %copy-start = (f32[27,1,8192]{2,0,1:T(8,128)S(1)}, f32[27,1,8192]{2,0,1:T(8,128)}, u32[]{:S(2)}) copy-start(f32[27,1,8192]{2,0,1:T(8,128)} %reduce-scatter.2.cloned.1.call-done) | copy-start | bytes 2654212
  231.8 51.7 %all-to-all-start.3 = ((bf16[8,2,1,8,8192]{4,1,0,2,3:T(2,128)(2,1)}), bf16[8,2,1,8,8192]{4,1,0,2,3:T(2,128)(2,1)S(1)}, u32[]{:S(2)}, u32[]{:S(2)}) async-start(bf16[8,2,1,8,8192]{4,1,0,2,3:T(2,128)(2,1)} %copy.39), calls=%async_computation.4 | async-start | bytes 4194304 | tf_op jit(solution)/shard_map/all_to_all | solution.py:111
Sparse Core Ops, SparseCore 0:
  12.7 47.2 reduce-scatter.1
